TPU v7x, 256 devices: a whole 4x4x8 slice. The times are simulated.
256 devices in a mesh: row: 2 (over core), col: 2 (over x_lo), rhs: 64 (over z, y, x_hi).
Axes of the slice: x: 4 (x_hi: 2, x_lo: 2; x = x_hi * 2 + x_lo), y: 4, z: 8, core: 2. Of those that a mesh axis runs over, the one named last changes fastest.
Arguments:
- front: bfloat16 [4096, 4096], P(('row', 'rhs'), 'col'), as said below
- anc_weight: bfloat16 [1024, 4096], P(('row', 'rhs'), 'col'), may hold values from -0.1875 to 0.1875
- solved: bfloat16 [2048, 8192], P(('row', 'col'), 'rhs'), may hold values from -6 to 6
- owners: int32 [8], replicated, may hold values from 0 to 3, as said below
- indices: int32 [8, 128], replicated, may hold values from 0 to 511
- counts: int32 [8], replicated, may hold values from 64 to 128, as said below
- rhs_side: bfloat16 [4096, 8192], P('row', 'rhs'), may hold values from -6 to 6
Outputs:
- solution: bfloat16 [4096, 8192], P('row', 'rhs')
Inputs may be any that keep to these rules, and one draw needn't show every extreme that they name: `front`: zero above the diagonal; diagonal entries 1 or more. The 4 tiles of each aligned block of 4 tiles have 4 different owners, numbered row index times 2 plus col index. `counts`: rows at or past a tile's count are padding.
All inputs are finite; a program needn't handle non-finite values.
Results may differ from a plain program's by a relative error of at most 0.0038.
Values may be sent and summed in bfloat16 or wider, within the bound.
No kernel may reach another device: no remote copies, remote signals or barrier semaphores. Data moves between devices by JAX's collectives and lax.ppermute only.
A program may use at most 128 MiB of HBM per device.

v0:
```python
import jax
import jax.numpy as jnp
from jax import lax
from jax.sharding import PartitionSpec as P


def from_root(x, axis, root):
    mine = lax.axis_index(axis) == root
    return lax.psum(jnp.where(mine, x, jnp.zeros_like(x)), axis)


def on_device(front, anc_weight, solved, owners, indices, counts, rhs_side):
    row_count = lax.axis_size("row")
    col_count = lax.axis_size("col")
    tiles_block = row_count * col_count
    row_index = lax.axis_index("row")
    col_index = lax.axis_index("col")
    tile_rows = indices.shape[1]
    columns = solved.shape[1]
    self_id = row_index * col_count + col_index
    owner_grid = owners.reshape(row_count, tiles_block)
    mine = (owner_grid == self_id).astype(jnp.int32)
    position = jnp.sum(mine * jnp.arange(tiles_block, dtype=jnp.int32)[None, :], axis=1)
    tile_ids = jnp.arange(row_count, dtype=jnp.int32) * tiles_block + position
    local_rows = indices[tile_ids]
    live_rows = jnp.arange(tile_rows, dtype=jnp.int32)[None, :] < counts[tile_ids][:, None]
    picked = solved[local_rows.reshape(-1)].reshape(row_count, tile_rows, columns)
    picked = jnp.where(live_rows[:, :, None], picked, jnp.zeros_like(picked))
    block_owners = lax.dynamic_slice_in_dim(owners, row_index * tiles_block, tiles_block)
    outgoing = jnp.broadcast_to(picked[:, None], (row_count, col_count, tile_rows, columns))
    outgoing = outgoing.reshape(row_count * col_count * tile_rows, columns)
    received = lax.all_to_all(outgoing, ("row", "col"), split_axis=0, concat_axis=0, tiled=True)
    slot_rows = received.reshape(tiles_block, tile_rows, columns)
    anc_values = slot_rows[block_owners].reshape(tiles_block * tile_rows, columns)
    front_tile = lax.all_gather(front, "rhs", axis=0, tiled=True)
    width = front_tile.shape[1]
    anc_total = lax.dot_general(
        lax.all_gather(anc_weight, "rhs", axis=0, tiled=True),
        anc_values,
        (((0,), (0,)), ((), ())),
        preferred_element_type=jnp.float32,
    )
    rhs_values = rhs_side.astype(jnp.float32)
    solution_rows = jnp.zeros((width, columns), jnp.bfloat16)
    for step_index in reversed(range(row_count)):
        current = solution_rows

        def no_product():
            return jnp.zeros((width, columns), jnp.float32)

        wanted = jnp.logical_and(col_index == step_index, row_index > step_index)

        def front_product():
            return lax.dot_general(
                front_tile, current, (((0,), (0,)), ((), ())), preferred_element_type=jnp.float32
            )

        front_term = lax.cond(wanted, front_product, no_product)
        rounded = lax.optimization_barrier((anc_total + front_term).astype(jnp.bfloat16))
        shares = lax.all_gather(rounded[None], "row", axis=0, tiled=True)
        summed = jnp.sum(shares.astype(jnp.float32), axis=0)
        reduced = rhs_values - summed

        def solve_block():
            return jax.scipy.linalg.solve_triangular(
                front_tile.astype(jnp.float32), reduced, trans=1, lower=True
            )

        on_diagonal = jnp.logical_and(row_index == step_index, col_index == step_index)
        fresh = lax.cond(on_diagonal, solve_block, no_product).astype(jnp.bfloat16)
        shared = from_root(fresh, "col", row_index)
        solution_rows = jnp.where(row_index == step_index, shared, solution_rows)
    return solution_rows


def solution(mesh):
    placed = (
        P(("row", "rhs"), "col"),
        P(("row", "rhs"), "col"),
        P(("row", "col"), "rhs"),
        P(),
        P(),
        P(),
        P("row", "rhs"),
    )
    return jax.shard_map(
        on_device, mesh=mesh, in_specs=placed, out_specs=P("row", "rhs"), check_vma=False
    )
```

profile of v0, /device:TPU:1, one launch (start us, length us, event | category | flops | bytes accessed | tf_op | source)
XLA Modules:
  0.0 989.0 jit_solution(2549492993331266399)
XLA Ops:
  6.5 0.0 copy-start
  6.5 0.0 copy-start.4
  6.5 0.0 all-gather.7.cloned.1.call-start
  6.5 0.7 all-gather.7.cloned.1.call-update
  7.3 0.0 all-gather.9.cloned.1.call-start
  7.3 0.7 all-gather.9.cloned.1.call-update
  8.0 0.7 broadcast_compare_fusion
  8.7 0.1 eq.34
  8.8 0.1 select_reduce_fusion
  8.9 1.2 gather_fusion.1
  10.2 1.3 gather_fusion
  11.5 0.0 copy-done
  11.5 0.9 gather_fusion.2
  12.3 0.1 iota_compare_fusion.2
  12.4 0.1 broadcast_select_fusion.4
  12.5 0.7 broadcast_in_dim.20
  13.2 6.5 all-to-all-start
  19.7 0.0 all-gather.11.cloned.1.call-start
  19.7 0.7 compare_select_fusion.1
  20.4 2.8 all-to-all-done
  23.2 0.6 gather_fusion.3
  23.8 137.7 %all-gather.7.cloned.1.call-done = bf16[2048,2048]{1,0:T(8,128)(2,1)} async-done(((bf16[32,2048]{1,0:T(8,128)(2,1)}), bf16[2048,2048]{1,0:T(8,128)(2,1)}) %all-gather.7.cloned.1.call-update) | async-done | bytes 8388624 | tf_op jit(solution)/shard_map/all_gather | solution.py:35
  161.5 0.1 conditional.4
  161.5 0.1 broadcast.102
  161.6 118.2 %all-gather.9.cloned.1.call-done = bf16[512,2048]{1,0:T(8,128)(2,1)} async-done(((bf16[8,2048]{1,0:T(8,128)(2,1)}), bf16[512,2048]{1,0:T(8,128)(2,1)}) %all-gather.9.cloned.1.call-update) | async-done | bytes 2097168 | tf_op jit(solution)/shard_map/all_gather | solution.py:38
  279.8 3.2 add_convert_fusion.1
  283.0 0.0 all-gather.11.cloned.1.call-update
  283.0 0.0 all-reduce.3.cloned.1.call-start
  283.1 0.0 copy-done.4
  283.1 0.1 convert_element_type.52
  283.2 15.7 %all-gather.11.cloned.1.call-done = bf16[4096,128]{0,1:T(8,128)(2,1)} async-done(((bf16[2048,128]{0,1:T(8,128)(2,1)}), bf16[4096,128]{0,1:T(8,128)(2,1)}) %all-gather.11.cloned.1.call-update) | async-done | bytes 1048592 | tf_op jit(solution)/shard_map/all_gather | solution.py:60
  298.8 1.4 convert_element_type.55
  300.3 5.8 conditional.5
  300.3 0.9 broadcast.104
  306.1 0.8 broadcast_select_fusion.2
  306.9 0.0 all-reduce.3.cloned.1.call-update
  306.9 0.0 all-gather.13.cloned.1.call-start
  307.0 320.4 %all-reduce.3.cloned.1.call-done = bf16[2048,128]{1,0:T(8,128)(2,1)} async-done(((bf16[2048,128]{1,0:T(8,128)(2,1)}), bf16[2048,128]{1,0:T(8,128)(2,1)}) %all-reduce.3.cloned.1.call-update) | async-done | bytes 524304 | tf_op jit(solution)/shard_map/psum | solution.py:9
  627.4 1.1 broadcast_select_fusion
  628.5 4.7 conditional.6
  628.5 4.7 fusion.103
  633.2 2.1 add_convert_fusion
  635.4 0.0 all-gather.13.cloned.1.call-update
  635.4 0.0 all-reduce.5.cloned.1.call-start
  635.4 15.7 %all-gather.13.cloned.1.call-done = bf16[4096,128]{0,1:T(8,128)(2,1)} async-done(((bf16[2048,128]{0,1:T(8,128)(2,1)}), bf16[4096,128]{0,1:T(8,128)(2,1)}) %all-gather.13.cloned.1.call-update) | async-done | bytes 1048592 | tf_op jit(solution)/shard_map/all_gather | solution.py:60
  651.1 1.4 convert_element_type.56
  652.5 2.0 conditional.7
  652.5 0.9 broadcast.106
  654.5 0.0 copy-start.1
  654.5 0.8 broadcast_select_fusion.1
  655.4 0.0 all-reduce.5.cloned.1.call-update
  655.4 324.6 %all-reduce.5.cloned.1.call-done = bf16[2048,128]{1,0:T(8,128)(2,1)} async-done(((bf16[2048,128]{1,0:T(8,128)(2,1)}), bf16[2048,128]{1,0:T(8,128)(2,1)}) %all-reduce.5.cloned.1.call-update) | async-done | bytes 524304 | tf_op jit(solution)/shard_map/psum | solution.py:9
  980.0 1.9 broadcast_select_fusion.3
  981.9 0.0 copy-done.1
  (5 shorter events, 0.0 us)
Async XLA Ops:
  6.5 4.9 copy-start
  6.5 276.5 %copy-start.4 = (bf16[2048,128]{1,0:T(8,128)(2,1)S(1)}, bf16[2048,128]{1,0:T(8,128)(2,1)}, u32[]{:S(2)}) copy-start(bf16[2048,128]{1,0:T(8,128)(2,1)} %param.23) | copy-start | bytes 1572868
  6.5 155.0 %all-gather.7.cloned.1.call-start = ((), (), s32[]{:S(2)}) async-start(), calls=%async_computation.1 | async-start | bytes 8519680 | tf_op jit(solution)/shard_map/all_gather | solution.py:35
  7.3 272.5 %all-gather.9.cloned.1.call-start = ((), (), s32[]{:S(2)}) async-start(), calls=%async_computation.2 | async-start | bytes 2129920 | tf_op jit(solution)/shard_map/all_gather | solution.py:38
  13.2 10.1 %all-to-all-start = ((bf16[4,128,128]{2,1,0:T(8,128)(2,1)}), bf16[4,128,128]{2,1,0:T(8,128)(2,1)S(1)}, u32[]{:S(2)}, u32[]{:S(2)}) async-start(bf16[4,128,128]{2,1,0:T(8,128)(2,1)} %bitcast.38), calls=%async_computation | async-start | bytes 262144 | tf_op jit(solution)/shard_map/all_to_all | solution.py:32
  19.7 279.2 %all-gather.11.cloned.1.call-start = ((), (), s32[]{:S(2)}) async-start(), calls=%async_computation.5 | async-start | bytes 1572864 | tf_op jit(solution)/shard_map/all_gather | solution.py:60
  283.0 344.4 %all-reduce.3.cloned.1.call-start = ((), (), s32[]{:S(2)}) async-start(), calls=%async_computation.3 | async-start | bytes 1048576 | tf_op jit(solution)/shard_map/psum | solution.py:9
  306.9 344.2 %all-gather.13.cloned.1.call-start = ((), (), s32[]{:S(2)}) async-start(), calls=%async_computation.6 | async-start | bytes 1572864 | tf_op jit(solution)/shard_map/all_gather | solution.py:60
  635.4 344.6 %all-reduce.5.cloned.1.call-start = ((), (), s32[]{:S(2)}) async-start(), calls=%async_computation.4 | async-start | bytes 1048576 | tf_op jit(solution)/shard_map/psum | solution.py:9
  654.5 327.4 %copy-start.1 = (bf16[512,128]{1,0:T(8,128)(2,1)S(1)}, bf16[512,128]{1,0:T(8,128)(2,1)}, u32[]{:S(2)}) copy-start(bf16[512,128]{1,0:T(8,128)(2,1)} %param.19) | copy-start | bytes 393220
Sparse Core Ops, SparseCore 0:
  10.8 150.6 all-gather.6
  165.1 114.6 all-gather.8
  283.1 15.6 all-gather.10
  307.0 320.3 all-reduce.2
  635.5 15.5 all-gather.12
  655.5 324.4 all-reduce.4
where the time goes:
time: 996 us; the launch traced here: 989 us
  waiting for transfers between devices  937 us (94%)
  between operations  13.9 us (1%)
  other arithmetic  11.4 us (1%)
    psum x2, waiting for transfers between devices, from_root(): return lax.psum(jnp.where(mine, x, jnp.zeros_like(x)), axis)  645 us
    all_gather x1, waiting for transfers between devices, on_device(): front_tile = lax.all_gather(front, 'rhs', axis=0, tiled=True)  138 us
    all_gather x1, waiting for transfers between devices, on_device(): lax.all_gather(anc_weight, 'rhs', axis=0, tiled=True)  118 us
    all_gather x2, waiting for transfers between devices, on_device(): shares = lax.all_gather(rounded[None], 'row', axis=0, tiled=True)  31.3 us
  transfers between devices with their start and end apart: 7, of which 7 were waited for; matrix products, arithmetic and copies ran while one was open for 1% of the time, Pallas kernels for 0%

commit v1 on v0

--- a/solution.py
+++ b/solution.py
@@ -32,7 +32,9 @@
     received = lax.all_to_all(outgoing, ("row", "col"), split_axis=0, concat_axis=0, tiled=True)
     slot_rows = received.reshape(tiles_block, tile_rows, columns)
     anc_values = slot_rows[block_owners].reshape(tiles_block * tile_rows, columns)
-    front_tile = lax.all_gather(front, "rhs", axis=0, tiled=True)
+    front_tile = jnp.concatenate(
+        lax.all_to_all(jnp.stack([front] * lax.axis_size("rhs")), "rhs", 0, 0), axis=0
+    )
     width = front_tile.shape[1]
     anc_total = lax.dot_general(
         lax.all_gather(anc_weight, "rhs", axis=0, tiled=True),

time: 996 us -> 948 us (0.952)
  waiting for transfers between devices: 937 us -> 868 us
    all_to_all x1, waiting for transfers between devices: 2.82 us -> 192 us  [on_device(): lax.all_to_all(jnp.stack([front] * lax.axis_size('rhs')), 'rhs', 0, 0)]
    all_gather x1 -> x0, waiting for transfers between devices: 138 us -> none  [on_device(): front_tile = lax.all_gather(front, 'rhs', axis=0, tiled=True)]
    all_gather x1, waiting for transfers between devices: 118 us -> 0.02 us  [on_device(): lax.all_gather(anc_weight, 'rhs', axis=0, tiled=True)]
  transfers between devices with their start and end apart: 7 -> 6, of which waited for: 7 -> 5; matrix products, arithmetic and copies ran while one was open for 1% -> 0% of each run, Pallas kernels for 0% -> 0%
where the time goes in v1:
time: 948 us; the launch traced here: 940 us
  waiting for transfers between devices  868 us (92%)
  between operations  13.6 us (1%)
  starting transfers between devices  13.2 us (1%)
  local copies, waits for them, and re-layouts  11.2 us (1%)
  other arithmetic  10.8 us (1%)
    psum x2, waiting for transfers between devices, from_root(): return lax.psum(jnp.where(mine, x, jnp.zeros_like(x)), axis)  644 us
    all_to_all x1, waiting for transfers between devices, on_device(): lax.all_to_all(jnp.stack([front] * lax.axis_size('rhs')), 'rhs', 0, 0)  192 us
    all_gather x2, waiting for transfers between devices, on_device(): shares = lax.all_gather(rounded[None], 'row', axis=0, tiled=True)  31.4 us
  transfers between devices with their start and end apart: 6, of which 5 were waited for; matrix products, arithmetic and copies ran while one was open for 0% of the time, Pallas kernels for 0%

profile of v1, /device:TPU:1, one launch (start us, length us, event | category | flops | bytes accessed | tf_op | source)
XLA Modules:
  0.0 939.9 jit_solution(4460553311709234009)
XLA Ops:
  6.5 0.0 copy-start
  6.5 0.0 copy-start.5
  6.5 0.7 broadcast_compare_fusion
  7.3 0.1 eq.34
  7.4 0.1 select_reduce_fusion
  7.5 1.2 gather_fusion.1
  8.8 1.3 gather_fusion
  10.1 0.1 iota_compare_fusion.2
  10.1 0.0 copy-done
  10.1 0.9 gather_fusion.2
  11.0 0.1 broadcast_select_fusion.4
  11.1 9.1 all_to_all.14
  20.3 5.3 stack.2
  25.5 0.0 copy-start.4
  25.5 13.0 %all-to-all-start = ((bf16[64,32,2048]{2,1,0:T(8,128)(2,1)}), bf16[64,32,2048]{2,1,0:T(8,128)(2,1)}, u32[]{:S(2)}, u32[]{:S(2)}) async-start(bf16[64,32,2048]{2,1,0:T(8,128)(2,1)} %stack.2), calls=%async_computation | async-start | bytes 16777216 | tf_op jit(solution)/shard_map/all_to_all | solution.py:36
  38.5 0.0 all-gather.6.cloned.1.call-start
  38.6 0.7 all-gather.6.cloned.1.call-update
  39.3 0.0 all-gather.8.cloned.1.call-start
  39.3 0.0 copy-done.5
  39.3 0.1 compare_select_fusion.1
  39.4 0.6 gather_fusion.3
  40.0 192.1 %all-to-all-done = bf16[64,32,2048]{2,1,0:T(8,128)(2,1)} async-done(((bf16[64,32,2048]{2,1,0:T(8,128)(2,1)}), bf16[64,32,2048]{2,1,0:T(8,128)(2,1)}, u32[]{:S(2)}, u32[]{:S(2)}) %all-to-all-start) | async-done | bytes 8388640 | tf_op jit(solution)/shard_map/all_to_all | solution.py:36
  232.1 0.1 conditional.4
  232.1 0.1 broadcast.104
  232.2 0.0 all-gather.6.cloned.1.call-done
  232.2 3.2 add_convert_fusion.1
  235.4 0.0 all-gather.8.cloned.1.call-update
  235.4 0.0 all-reduce.3.cloned.1.call-start
  235.5 0.0 copy-done.4
  235.5 0.1 convert_element_type.52
  235.6 15.7 %all-gather.8.cloned.1.call-done = bf16[4096,128]{0,1:T(8,128)(2,1)} async-done(((bf16[2048,128]{0,1:T(8,128)(2,1)}), bf16[4096,128]{0,1:T(8,128)(2,1)}) %all-gather.8.cloned.1.call-update) | async-done | bytes 1048592 | tf_op jit(solution)/shard_map/all_gather | solution.py:62
  251.3 1.4 convert_element_type.55
  252.8 5.8 conditional.5
  252.8 0.9 broadcast.106
  258.5 0.8 broadcast_select_fusion.2
  259.4 0.0 all-reduce.3.cloned.1.call-update
  259.4 0.0 all-gather.10.cloned.1.call-start
  259.5 319.8 %all-reduce.3.cloned.1.call-done = bf16[2048,128]{1,0:T(8,128)(2,1)} async-done(((bf16[2048,128]{1,0:T(8,128)(2,1)}), bf16[2048,128]{1,0:T(8,128)(2,1)}) %all-reduce.3.cloned.1.call-update) | async-done | bytes 524304 | tf_op jit(solution)/shard_map/psum | solution.py:9
  579.3 1.1 broadcast_select_fusion
  580.4 4.7 conditional.6
  580.4 4.7 fusion.103
  585.1 2.1 add_convert_fusion
  587.2 0.0 all-gather.10.cloned.1.call-update
  587.2 0.0 all-reduce.5.cloned.1.call-start
  587.3 15.7 %all-gather.10.cloned.1.call-done = bf16[4096,128]{0,1:T(8,128)(2,1)} async-done(((bf16[2048,128]{0,1:T(8,128)(2,1)}), bf16[4096,128]{0,1:T(8,128)(2,1)}) %all-gather.10.cloned.1.call-update) | async-done | bytes 1048592 | tf_op jit(solution)/shard_map/all_gather | solution.py:62
  602.9 1.4 convert_element_type.56
  604.4 2.0 conditional.7
  604.4 0.9 broadcast.108
  606.3 0.0 copy-start.1
  606.4 0.8 broadcast_select_fusion.1
  607.2 0.0 all-reduce.5.cloned.1.call-update
  607.2 324.0 %all-reduce.5.cloned.1.call-done = bf16[2048,128]{1,0:T(8,128)(2,1)} async-done(((bf16[2048,128]{1,0:T(8,128)(2,1)}), bf16[2048,128]{1,0:T(8,128)(2,1)}) %all-reduce.5.cloned.1.call-update) | async-done | bytes 524304 | tf_op jit(solution)/shard_map/psum | solution.py:9
  931.2 1.9 broadcast_select_fusion.3
  933.1 0.0 copy-done.1
  (6 shorter events, 0.1 us)
Async XLA Ops:
  6.5 3.6 copy-start
  6.5 32.8 %copy-start.5 = (s32[8]{0:T(128)S(1)}, s32[8]{0:T(128)}, u32[]{:S(2)}) copy-start(s32[8]{0:T(128)} %param.20) | copy-start | bytes 100
  25.5 210.0 %copy-start.4 = (bf16[2048,128]{1,0:T(8,128)(2,1)S(1)}, bf16[2048,128]{1,0:T(8,128)(2,1)}, u32[]{:S(2)}) copy-start(bf16[2048,128]{1,0:T(8,128)(2,1)} %param.23) | copy-start | bytes 1572868
  25.5 206.5 %all-to-all-start = ((bf16[64,32,2048]{2,1,0:T(8,128)(2,1)}), bf16[64,32,2048]{2,1,0:T(8,128)(2,1)}, u32[]{:S(2)}, u32[]{:S(2)}) async-start(bf16[64,32,2048]{2,1,0:T(8,128)(2,1)} %stack.2), calls=%async_computation | async-start | bytes 16777216 | tf_op jit(solution)/shard_map/all_to_all | solution.py:36
  38.5 193.7 %all-gather.6.cloned.1.call-start = ((), (), s32[]{:S(2)}) async-start(), calls=%async_computation.2 | async-start | bytes 2129920 | tf_op jit(solution)/shard_map/all_gather | solution.py:40
  39.3 212.1 %all-gather.8.cloned.1.call-start = ((), (), s32[]{:S(2)}) async-start(), calls=%async_computation.5 | async-start | bytes 1572864 | tf_op jit(solution)/shard_map/all_gather | solution.py:62
  235.4 343.8 %all-reduce.3.cloned.1.call-start = ((), (), s32[]{:S(2)}) async-start(), calls=%async_computation.3 | async-start | bytes 1048576 | tf_op jit(solution)/shard_map/psum | solution.py:9
  259.4 343.5 %all-gather.10.cloned.1.call-start = ((), (), s32[]{:S(2)}) async-start(), calls=%async_computation.6 | async-start | bytes 1572864 | tf_op jit(solution)/shard_map/all_gather | solution.py:62
  587.2 344.0 %all-reduce.5.cloned.1.call-start = ((), (), s32[]{:S(2)}) async-start(), calls=%async_computation.4 | async-start | bytes 1048576 | tf_op jit(solution)/shard_map/psum | solution.py:9
  606.3 326.8 %copy-start.1 = (bf16[512,128]{1,0:T(8,128)(2,1)S(1)}, bf16[512,128]{1,0:T(8,128)(2,1)}, u32[]{:S(2)}) copy-start(bf16[512,128]{1,0:T(8,128)(2,1)} %param.19) | copy-start | bytes 393220
Sparse Core Ops, SparseCore 0:
  42.9 163.9 all-gather.5
  235.5 15.7 all-gather.7
  259.5 319.6 all-reduce.2
  587.3 15.5 all-gather.9
  607.3 323.8 all-reduce.4
